TPU v7x, 32 devices: a whole 2x2x4 slice. The times are simulated.
32 devices in a mesh: grp: 1, seq: 4 (over z), dp: 4 (over y, x), head: 2 (over core).
Axes of the slice: x: 2, y: 2, z: 4, core: 2. Of those that a mesh axis runs over, the one named last changes fastest.
Arguments:
- tokens_in: bfloat16 [4, 1024, 4096], P(('grp', 'dp'), 'seq'), may hold values from -6 to 6
- positions: int32 [4, 1024], P(('grp', 'dp'), 'seq'), may hold values from 0 to 1023, as said below
- doc_start: int32 [4, 1024], P(('grp', 'dp'), 'seq'), may hold values from 0 to 1, as said below
- feature_weight: bfloat16 [4096, 4096], P(('seq', 'dp'), 'head'), may hold values from -0.09375 to 0.09375
- state_weight: bfloat16 [4096, 128], P(('seq', 'dp')), may hold values from -0.01171875 to 0.01171875
- step_weight: bfloat16 [4096, 32], P(('seq', 'dp'), 'head'), may hold values from -0.09375 to 0.09375
- step_bias: float32 [32], P('head'), may hold values from -1 to 0.5
- decay_log: float32 [32], P('head')
- skip_gain: float32 [32], P('head'), may hold values from 0.4 to 1.9
- norm_gain: float32 [4096], P('head'), may hold values from 0.5 to 1.5
Outputs:
- mixed: bfloat16 [4, 1024, 4096], P(('grp', 'dp'), 'seq', 'head')
Inputs may be any that keep to these rules, and one draw needn't show every extreme that they name: Each sequence's rows carry every position once. Cut each device's 256 rows into 4 equal slots in order: the positions of slot k all lie in [k * 256, (k + 1) * 256). `doc_start`: position 0 of every sequence holds 1; a sequence holds at most 4 ones.
All inputs are finite; a program needn't handle non-finite values.
Results may differ from a plain program's by a relative error of at most 0.0062.
Values may be sent and summed in bfloat16 or wider, within the bound.
No kernel may reach another device: no remote copies, remote signals or barrier semaphores. Data moves between devices by JAX's collectives and lax.ppermute only.
A program may use at most 128 MiB of HBM per device.

v0:
```python
import jax
import jax.numpy as jnp
from jax import lax
from jax.sharding import PartitionSpec as P

HIGH = lax.Precision.HIGHEST


def carried(gain, state, axis, reverse):
    count = lax.axis_size(axis)
    here = lax.axis_index(axis)
    rows = state.shape[0] * state.shape[1]
    pad = jnp.zeros((8, state.shape[2]), state.dtype).at[0, : gain.shape[0]].set(gain)
    value = jnp.concatenate([state.reshape(rows, -1), pad])

    def shift(x, step):
        if reverse:
            pairs = [(j, j - step) for j in range(step, count)]
            reached = here < count - step
        else:
            pairs = [(j, j + step) for j in range(count - step)]
            reached = here >= step
        return (lax.ppermute(x, axis, pairs), reached)

    value, reached = shift(value, 1)
    value = value.at[rows].set(jnp.where(reached, value[rows], 1.0))
    step = 1
    while step < count:
        earlier, reached = shift(value, step)
        g_early = jnp.where(reached, earlier[rows, : gain.shape[0]], 1.0)
        g_late = value[rows, : gain.shape[0]]
        late = value[:rows].reshape(state.shape)
        merged = g_late[:, None, None] * earlier[:rows].reshape(state.shape) + late
        value = jnp.concatenate(
            [merged.reshape(rows, -1), value[rows:].at[0, : gain.shape[0]].set(g_early * g_late)]
        )
        step *= 2
    return value[:rows].reshape(state.shape)


def per_device(
    tokens_in,
    positions,
    doc_start,
    feature_weight,
    state_weight,
    step_weight,
    step_bias,
    decay_log,
    skip_gain,
    norm_gain,
):
    row_count = tokens_in.shape[1]
    shards = lax.axis_size("seq")
    here = lax.axis_index("seq")
    slot = row_count // shards
    head_count = step_bias.shape[0]
    feat_cols = feature_weight.shape[1]
    head_size = feat_cols // head_count
    state_size = state_weight.shape[1] // 2
    seq_count = lax.axis_size("seq")
    dp_count = lax.axis_size("dp")
    block_rows = feature_weight.shape[0]
    weights = jnp.concatenate([feature_weight, state_weight, step_weight], axis=1)
    gathered = lax.all_gather(weights, "seq", axis=0, tiled=True)
    parts = tokens_in[0].reshape(row_count, seq_count, dp_count, block_rows).transpose(2, 0, 1, 3)
    mine = lax.all_to_all(parts, "dp", 0, 0, tiled=True)
    mine = mine.reshape(dp_count * row_count, seq_count * block_rows)
    partial = jnp.dot(mine, gathered, preferred_element_type=jnp.float32)
    projected = lax.psum_scatter(partial, "dp", scatter_dimension=0, tiled=True)
    projected = projected.astype(jnp.bfloat16).reshape(shards, slot, -1)
    moved = lax.all_to_all(projected, "seq", 0, 0, tiled=True).reshape(row_count, -1)
    moved_positions = lax.all_to_all(
        positions[0].reshape(shards, slot), "seq", 0, 0, tiled=True
    ).reshape(row_count)
    offsets = moved_positions - here * row_count
    inverse = (
        jnp.zeros((row_count,), jnp.int32).at[offsets].set(jnp.arange(row_count, dtype=jnp.int32))
    )
    proj = moved[inverse]
    x_proj = proj[:, :feat_cols]
    bc_proj = proj[:, feat_cols : feat_cols + 2 * state_size]
    step_raw = proj[:, feat_cols + 2 * state_size :]
    b_float = bc_proj[:, :state_size].astype(jnp.float32)
    c_float = bc_proj[:, state_size:].astype(jnp.float32)
    step_size = jax.nn.softplus(step_raw.astype(jnp.float32) + step_bias[None, :])
    log_decay = -jnp.exp(decay_log)[None, :] * step_size
    cum_decay = jnp.cumsum(log_decay, axis=0)
    doc_index = jnp.cumsum(doc_start[0], axis=0)
    scores = jnp.dot(
        bc_proj[:, state_size:], bc_proj[:, :state_size].T, preferred_element_type=jnp.float32
    )
    places = jnp.arange(row_count, dtype=jnp.int32)
    same_doc = (
        (doc_index[:, None] == doc_index[None, :]) & (places[:, None] != places[None, :])
    ).astype(jnp.float32)
    cum_t = cum_decay.T
    step_t = step_size.T
    decay = jnp.exp(-jnp.abs(cum_t[:, :, None] - cum_t[:, None, :])) * same_doc[None]
    mixing = scores[None] * decay * step_t[:, None, :]
    x_heads = x_proj.reshape(row_count, head_count, head_size).astype(jnp.float32)
    y_local = jnp.einsum("hts,shp->thp", mixing, x_heads, precision=HIGH)
    last_doc = (doc_index == doc_index[-1]).astype(jnp.float32)
    first_doc = (doc_index == 0).astype(jnp.float32)
    end_weight = jnp.exp(cum_decay[-1][None, :] - cum_decay) * last_doc[:, None] * step_size
    begin_weight = jnp.exp(cum_decay) * first_doc[:, None] * step_size
    state_end = jnp.einsum("tn,th,thp->hnp", b_float, end_weight, x_heads, precision=HIGH)
    state_begin = jnp.einsum("tn,th,thp->hnp", b_float, begin_weight, x_heads, precision=HIGH)
    carry_gain = jnp.exp(cum_decay[-1]) * (doc_index[-1] == 0)
    prefix = carried(carry_gain, state_end, "seq", False)
    suffix = carried(carry_gain, state_begin, "seq", True)
    left_gate = jnp.exp(cum_decay) * first_doc[:, None]
    right_gate = jnp.exp(cum_decay[-1][None, :] - cum_decay) * last_doc[:, None]
    from_left = jnp.einsum("tn,hnp->thp", c_float, prefix, precision=HIGH)
    from_right = jnp.einsum("tn,hnp->thp", c_float, suffix, precision=HIGH)
    mixer = (
        y_local
        + left_gate[:, :, None] * from_left
        + right_gate[:, :, None] * from_right
        + skip_gain[None, :, None] * x_heads
    )
    mixer_rows = mixer.reshape(row_count, head_count * head_size)
    square_sum = lax.psum(jnp.sum(mixer_rows * mixer_rows, axis=1), "head")
    full_width = mixer_rows.shape[1] * lax.axis_size("head")
    inv_scale = lax.rsqrt(square_sum / full_width + 1e-05)
    return (mixer_rows * inv_scale[:, None] * norm_gain[None, :]).astype(jnp.bfloat16)[None]


def solution(mesh):
    placed = (
        P(("grp", "dp"), "seq", None),
        P(("grp", "dp"), "seq"),
        P(("grp", "dp"), "seq"),
        P(("seq", "dp"), "head"),
        P(("seq", "dp"), None),
        P(("seq", "dp"), "head"),
        P("head"),
        P("head"),
        P("head"),
        P("head"),
    )
    return jax.shard_map(
        per_device,
        mesh=mesh,
        in_specs=placed,
        out_specs=P(("grp", "dp"), "seq", "head"),
        check_vma=False,
    )
```

profile of v0, /device:TPU:0, one launch (start us, length us, event | category | flops | bytes accessed | tf_op | source)
XLA Modules:
  0.0 328.3 jit_solution(13691790862936015671)
XLA Ops:
  7.4 2.4 pad_maximum_fusion
  9.8 3.3 %reshape_squeeze.4 = bf16[256,4,4,256]{3,2,1,0:T(4,128)(2,1)S(1)} reshape(bf16[1,256,4096]{2,1,0:T(8,128)(2,1)} %param.22) | data formatting | bytes 4194304 | tf_op jit(solution)/shard_map/reshape;squeeze | solution.py:66
  13.9 30.4 %all_to_all.19 = bf16[4,256,4,256]{3,2,1,0:T(4,128)(2,1)S(1)} all-to-all(bf16[4,256,4,256]{3,2,1,0:T(4,128)(2,1)S(1)} %bitcast.103), channel_id=1, replica_groups=mesh['grp'=1,'seq'=4,'dp'=4,'head'=2] {'dp'}, dimensions={0} | all-to-all | bytes 4194304 | tf_op jit(solution)/shard_map/all_to_all | solution.py:67
  44.8 57.2 %all-gather.2.cloned.1.call-done = bf16[1024,2192]{1,0:T(8,128)(2,1)} async-done(((bf16[256,2192]{1,0:T(8,128)(2,1)}), bf16[1024,2192]{1,0:T(8,128)(2,1)}) %all-gather.2.cloned.1.call-update) | async-done | bytes 4489232 | tf_op jit(solution)/shard_map/all_gather | solution.py:65
  102.0 10.0 %convolution_bitcast_fusion = f32[1024,2192]{0,1:T(8,128)} fusion(bf16[1024,2192]{1,0:T(8,128)(2,1)} %all-gather.2.cloned.1.call-done, bf16[1024,1024]{1,0:T(8,128)(2,1)S(1)} %bitcast.110), kind=kOutput, calls=%fused_computation.2 | convolution fusion | flops 4596957184 | bytes 15564800 | tf_op jit(solution)/shard_map/dot_general | solution.py:69
  114.0 3.2 all-to-all-start.2
  117.2 84.5 %reduce-scatter.2.cloned.1.call-done = f32[256,2192]{0,1:T(8,128)} async-done(((f32[1024,2192]{0,1:T(8,128)}), f32[256,2192]{0,1:T(8,128)}) %reduce-scatter.2.cloned.1.call-update) | async-done | bytes 2244624 | tf_op jit(solution)/shard_map/reduce_scatter | solution.py:70
  201.7 1.7 convert_element_type.43
  203.5 1.5 copy.77
  205.0 4.6 %all-to-all-start.1 = ((bf16[4,64,2192]{2,1,0:T(8,128)(2,1)}), bf16[4,64,2192]{2,1,0:T(8,128)(2,1)S(1)}, u32[]{:S(2)}, u32[]{:S(2)}) async-start(bf16[4,64,2192]{2,1,0:T(8,128)(2,1)} %bitcast.2), calls=%async_computation.2 | async-start | bytes 2359296 | tf_op jit(solution)/shard_map/all_to_all | solution.py:72
  213.7 24.3 %all-to-all-done.1 = bf16[4,64,2192]{2,1,0:T(8,128)(2,1)S(1)} async-done(((bf16[4,64,2192]{2,1,0:T(8,128)(2,1)}), bf16[4,64,2192]{2,1,0:T(8,128)(2,1)S(1)}, u32[]{:S(2)}, u32[]{:S(2)}) %all-to-all-start.1) | async-done | bytes 1122336 | tf_op jit(solution)/shard_map/all_to_all | solution.py:72
  238.0 1.4 gather_fusion
  247.7 4.6 %collective-permute-start = (f32[1032,128]{1,0:T(8,128)}, f32[1032,128]{1,0:T(8,128)S(1)}, u32[]{:S(2)}, u32[]{:S(2)}) collective-permute-start(f32[1032,128]{1,0:T(8,128)} %get-tuple-element.95), channel_id=1, source_target_pairs={{0,8},{8,16},{16,24},{1,9},{9,17},{17,25},{2,10},{10,18},{18,26},{... | collective-permute-start | bytes 1585160 | tf_op jit(solution)/shard_map/ppermute | solution.py:23
  253.4 8.2 %collective-permute-done.3 = f32[1032,128]{1,0:T(8,128)S(1)} collective-permute-done((f32[1032,128]{1,0:T(8,128)}, f32[1032,128]{1,0:T(8,128)S(1)}, u32[]{:S(2)}, u32[]{:S(2)}) %collective-permute-start.3) | collective-permute-done | bytes 528416 | tf_op jit(solution)/shard_map/ppermute | solution.py:23
  263.0 5.3 %collective-permute-start.1 = (f32[1032,128]{1,0:T(8,128)S(1)}, f32[1032,128]{1,0:T(8,128)}, u32[]{:S(2)}, u32[]{:S(2)}) collective-permute-start(f32[1032,128]{1,0:T(8,128)S(1)} %scatter.26), channel_id=1, source_target_pairs={{0,8},{8,16},{16,24},{1,9},{9,17},{17,25},{2,10},{10,18},{18,26},{... | collective-permute-start | bytes 1585160 | tf_op jit(solution)/shard_map/ppermute | solution.py:23
  268.3 5.7 %fusion = f32[16,128,256]{2,1,0:T(8,128)} fusion(bf16[256,16,128]{0,2,1:T(8,128)(2,1)S(1)} %bitcast.100, f32[16,256]{1,0:T(8,128)} %get-tuple-element.91, f32[256,256]{1,0:T(8,128)} %fusion.35, f32[16,256]{1,0:T(8,128)} %get-tuple-element.90, f32[256,256]{1,0:T(8,128)S(1)} %fusion.41), kind=kOutput, calls=%fused_computation.3 | convolution fusion | flops 1616904192 | bytes 3702784 | tf_op jit(solution)/shard_map/hts,shp->thp/dot_general | solution.py:102
  274.0 1.8 collective-permute-done.4
  280.1 5.0 %collective-permute-start.2 = (f32[1032,128]{1,0:T(8,128)}, f32[1032,128]{1,0:T(8,128)}, u32[]{:S(2)}, u32[]{:S(2)}) collective-permute-start(f32[1032,128]{1,0:T(8,128)} %pad_maximum_fusion.1), channel_id=1, source_target_pairs={{0,16},{8,24},{1,17},{9,25},{2,18},{10,26},{3,19},{11,27},{4,20},{... | collective-permute-start | bytes 1585160 | tf_op jit(solution)/shard_map/ppermute | solution.py:23
  289.3 4.2 %collective-permute-done.2 = f32[1032,128]{1,0:T(8,128)} collective-permute-done((f32[1032,128]{1,0:T(8,128)}, f32[1032,128]{1,0:T(8,128)}, u32[]{:S(2)}, u32[]{:S(2)}) %collective-permute-start.2) | collective-permute-done | bytes 528416 | tf_op jit(solution)/shard_map/ppermute | solution.py:23
  295.8 15.8 %collective-permute-done.5 = f32[1032,128]{1,0:T(8,128)S(1)} collective-permute-done((f32[1032,128]{1,0:T(8,128)S(1)}, f32[1032,128]{1,0:T(8,128)S(1)}, u32[]{:S(2)}, u32[]{:S(2)}) %collective-permute-start.5) | collective-permute-done | bytes 528416 | tf_op jit(solution)/shard_map/ppermute | solution.py:23
  311.7 2.6 multiply_reduce_fusion
  314.4 1.9 copy.88
  316.2 2.4 psum.7
  318.7 2.8 multiply_convert_fusion
  (97 shorter events, 29.0 us)
Async XLA Ops:
  6.5 95.5 %all-gather.2.cloned.1.call-start = ((), (), s32[]{:S(2)}) async-start(), calls=%async_computation.4 | async-start | bytes 5898240 | tf_op jit(solution)/shard_map/all_gather | solution.py:65
  9.7 192.0 %reduce-scatter.2.cloned.1.call-start = ((), (), s32[]{:S(2)}) async-start(), calls=%async_computation.5 | async-start | bytes 11223040 | tf_op jit(solution)/shard_map/reduce_scatter | solution.py:70
  112.0 0.7 copy-start.8
  114.0 91.0 %all-to-all-start.2 = ((s32[4,1,64]{2,1,0:T(1,128)}), s32[4,1,64]{2,1,0:T(1,128)S(1)}, u32[]{:S(2)}, u32[]{:S(2)}) async-start(s32[4,1,64]{2,1,0:T(1,128)} %all_to_all.14), calls=%async_computation.3 | async-start | bytes 4096 | tf_op jit(solution)/shard_map/all_to_all | solution.py:73
  203.5 6.2 %copy-start.9 = (s32[1,256]{1,0:T(1,128)S(1)}, s32[1,256]{1,0:T(1,128)}, u32[]{:S(2)}) copy-start(s32[1,256]{1,0:T(1,128)} %param.24) | copy-start | bytes 3076
  203.5 8.0 %copy-start.11 = (f32[16]{0:T(128)S(1)}, f32[16]{0:T(128)}, u32[]{:S(2)}) copy-start(f32[16]{0:T(128)} %param.29) | copy-start | bytes 196
  205.0 33.0 %all-to-all-start.1 = ((bf16[4,64,2192]{2,1,0:T(8,128)(2,1)}), bf16[4,64,2192]{2,1,0:T(8,128)(2,1)S(1)}, u32[]{:S(2)}, u32[]{:S(2)}) async-start(bf16[4,64,2192]{2,1,0:T(8,128)(2,1)} %bitcast.2), calls=%async_computation.2 | async-start | bytes 2359296 | tf_op jit(solution)/shard_map/all_to_all | solution.py:72
  239.4 55.2 %copy-start = (bf16[256,2192]{1,0:T(8,128)(2,1)}, bf16[256,2192]{1,0:T(8,128)(2,1)S(1)}, u32[]{:S(2)}) copy-start(bf16[256,2192]{1,0:T(8,128)(2,1)S(1)} %gather_fusion) | copy-start | bytes 3366916
  239.4 0.7 copy-start.7
  246.4 15.1 %collective-permute-start.3 = (f32[1032,128]{1,0:T(8,128)}, f32[1032,128]{1,0:T(8,128)S(1)}, u32[]{:S(2)}, u32[]{:S(2)}) collective-permute-start(f32[1032,128]{1,0:T(8,128)} %get-tuple-element.94), channel_id=1, source_target_pairs={{8,0},{16,8},{24,16},{9,1},{17,9},{25,17},{10,2},{18,10},{26,18},{... | collective-permute-start | bytes 1585160 | tf_op jit(solution)/shard_map/ppermute | solution.py:23
  247.7 15.2 %collective-permute-start = (f32[1032,128]{1,0:T(8,128)}, f32[1032,128]{1,0:T(8,128)S(1)}, u32[]{:S(2)}, u32[]{:S(2)}) collective-permute-start(f32[1032,128]{1,0:T(8,128)} %get-tuple-element.95), channel_id=1, source_target_pairs={{0,8},{8,16},{16,24},{1,9},{9,17},{17,25},{2,10},{10,18},{18,26},{... | collective-permute-start | bytes 1585160 | tf_op jit(solution)/shard_map/ppermute | solution.py:23
  261.6 12.4 %copy-start.3 = (f32[1032,128]{1,0:T(8,128)}, f32[1032,128]{1,0:T(8,128)S(1)}, u32[]{:S(2)}) copy-start(f32[1032,128]{1,0:T(8,128)S(1)} %scatter.30) | copy-start | bytes 1585156
  261.6 14.2 %collective-permute-start.4 = (f32[1032,128]{1,0:T(8,128)S(1)}, f32[1032,128]{1,0:T(8,128)}, u32[]{:S(2)}, u32[]{:S(2)}) collective-permute-start(f32[1032,128]{1,0:T(8,128)S(1)} %scatter.30), channel_id=1, source_target_pairs={{8,0},{16,8},{24,16},{9,1},{17,9},{25,17},{10,2},{18,10},{26,18},{... | collective-permute-start | bytes 1585160 | tf_op jit(solution)/shard_map/ppermute | solution.py:23
  263.0 11.0 %copy-start.2 = (f32[1032,128]{1,0:T(8,128)}, f32[1032,128]{1,0:T(8,128)S(1)}, u32[]{:S(2)}) copy-start(f32[1032,128]{1,0:T(8,128)S(1)} %scatter.26) | copy-start | bytes 1585156
  263.0 13.9 %collective-permute-start.1 = (f32[1032,128]{1,0:T(8,128)S(1)}, f32[1032,128]{1,0:T(8,128)}, u32[]{:S(2)}, u32[]{:S(2)}) collective-permute-start(f32[1032,128]{1,0:T(8,128)S(1)} %scatter.26), channel_id=1, source_target_pairs={{0,8},{8,16},{16,24},{1,9},{9,17},{17,25},{2,10},{10,18},{18,26},{... | collective-permute-start | bytes 1585160 | tf_op jit(solution)/shard_map/ppermute | solution.py:23
  280.1 13.4 %collective-permute-start.2 = (f32[1032,128]{1,0:T(8,128)}, f32[1032,128]{1,0:T(8,128)}, u32[]{:S(2)}, u32[]{:S(2)}) collective-permute-start(f32[1032,128]{1,0:T(8,128)} %pad_maximum_fusion.1), channel_id=1, source_target_pairs={{0,16},{8,24},{1,17},{9,25},{2,18},{10,26},{3,19},{11,27},{4,20},{... | collective-permute-start | bytes 1585160 | tf_op jit(solution)/shard_map/ppermute | solution.py:23
  286.7 25.0 %collective-permute-start.5 = (f32[1032,128]{1,0:T(8,128)S(1)}, f32[1032,128]{1,0:T(8,128)S(1)}, u32[]{:S(2)}, u32[]{:S(2)}) collective-permute-start(f32[1032,128]{1,0:T(8,128)S(1)} %pad_maximum_fusion.2), channel_id=1, source_target_pairs={{16,0},{24,8},{17,1},{25,9},{18,2},{26,10},{19,3},{27,11},{20,4},{... | collective-permute-start | bytes 1585160 | tf_op jit(solution)/shard_map/ppermute | solution.py:23
  294.6 17.1 %copy-start.1 = (f32[16,128,256]{2,1,0:T(8,128)S(1)}, f32[16,128,256]{2,1,0:T(8,128)}, u32[]{:S(2)}) copy-start(f32[16,128,256]{2,1,0:T(8,128)} %fusion) | copy-start | bytes 6291460
  294.6 17.1 %copy-start.4 = (f32[256,16]{0,1:T(8,128)S(1)}, f32[256,16]{0,1:T(8,128)}, u32[]{:S(2)}) copy-start(f32[256,16]{0,1:T(8,128)} %get-tuple-element.74) | copy-start | bytes 49156
  294.6 17.1 %copy-start.5 = (f32[256,16]{0,1:T(8,128)S(1)}, f32[256,16]{0,1:T(8,128)}, u32[]{:S(2)}) copy-start(f32[256,16]{0,1:T(8,128)} %get-tuple-element.86) | copy-start | bytes 49156
  294.6 17.1 %copy-start.10 = (f32[16]{0:T(128)S(1)}, f32[16]{0:T(128)}, u32[]{:S(2)}) copy-start(f32[16]{0:T(128)} %param.30) | copy-start | bytes 196
  314.4 4.3 %copy-start.6 = (f32[2048]{0:T(1024)S(1)}, f32[2048]{0:T(1024)}, u32[]{:S(2)}) copy-start(f32[2048]{0:T(1024)} %param.31) | copy-start | bytes 24580
Sparse Core Ops, SparseCore 0:
  9.9 92.0 all-gather.1
  112.1 89.5 reduce-scatter.1
where the time goes:
time: 329 us; the launch traced here: 328 us
  waiting for transfers between devices  196 us (60%)
  blocking collectives  32.8 us (10%)
  starting transfers between devices  26.7 us (8%)
  matrix products  22.3 us (7%)
  other arithmetic  19.3 us (6%)
  local copies, waits for them, and re-layouts  16.5 us (5%)
  between operations  14.4 us (4%)
    reduce_scatter x1, waiting for transfers between devices, per_device(): projected = lax.psum_scatter(partial, 'dp', scatter_dimension=0, tiled=True)  84.5 us
    all_gather x1, waiting for transfers between devices, per_device(): gathered = lax.all_gather(weights, 'seq', axis=0, tiled=True)  57.2 us
    all_to_all x1, blocking collectives, per_device(): mine = lax.all_to_all(parts, 'dp', 0, 0, tiled=True)  30.4 us
    ppermute x6, waiting for transfers between devices, shift(): return (lax.ppermute(x, axis, pairs), reached)  30.3 us
    all_to_all x1, waiting for transfers between devices, per_device(): lax.all_to_all(projected, 'seq', 0, 0, tiled=True).reshape(row_count, -1)  24.3 us
    ppermute x6, starting transfers between devices, shift(): return (lax.ppermute(x, axis, pairs), reached)  18.8 us
    dot_general x1, matrix products, per_device(): partial = jnp.dot(mine, gathered, preferred_element_type=jnp.float32)  9.96 us
  transfers between devices with their start and end apart: 10, of which 8 were waited for; matrix products, arithmetic and copies ran while one was open for 8% of the time, Pallas kernels for 0%

commit v1 on v0

--- a/solution.py
+++ b/solution.py
@@ -4,6 +4,29 @@
 from jax.sharding import PartitionSpec as P
 
 HIGH = lax.Precision.HIGHEST
+
+
+def in_blocks(array, dim, size):
+    lengths = array.shape
+    blocks = array.reshape(*lengths[:dim], size, lengths[dim] // size, *lengths[dim + 1 :])
+    return jnp.moveaxis(blocks, dim, 0)
+
+
+def joined_along(parts, dim):
+    dims = list(parts.shape[1:])
+    dims[dim] *= parts.shape[0]
+    return jnp.moveaxis(parts, 0, dim).reshape(dims)
+
+
+def pairwise_exchange(x, axis, split_dim, concat_dim):
+    size, index = (lax.axis_size(axis), lax.axis_index(axis))
+    pieces = in_blocks(x, split_dim, size)
+    finished = [pieces[index]]
+    for step in range(1, size):
+        sent = pieces[index ^ step]
+        finished.append(lax.ppermute(sent, axis, [(i, i ^ step) for i in range(size)]))
+    pieces = jnp.stack(finished)[index ^ jnp.arange(size)]
+    return joined_along(pieces, concat_dim)
 
 
 def carried(gain, state, axis, reverse):
@@ -69,7 +92,7 @@
     partial = jnp.dot(mine, gathered, preferred_element_type=jnp.float32)
     projected = lax.psum_scatter(partial, "dp", scatter_dimension=0, tiled=True)
     projected = projected.astype(jnp.bfloat16).reshape(shards, slot, -1)
-    moved = lax.all_to_all(projected, "seq", 0, 0, tiled=True).reshape(row_count, -1)
+    moved = pairwise_exchange(projected, "seq", 0, 0).reshape(row_count, -1)
     moved_positions = lax.all_to_all(
         positions[0].reshape(shards, slot), "seq", 0, 0, tiled=True
     ).reshape(row_count)

time: 329 us -> 325 us (0.988)
  waiting for transfers between devices: 196 us -> 192 us
    all_to_all x1 -> x0, waiting for transfers between devices: 24.3 us -> none  [per_device(): lax.all_to_all(projected, 'seq', 0, 0, tiled=True).reshape(row_count, -1)]
    ppermute x0 -> x3, waiting for transfers between devices: none -> 24.1 us  [pairwise_exchange(): lax.ppermute(sent, axis, [(i, i ^ step) for i in range(size)])]
    reduce_scatter x1, waiting for transfers between devices: 84.5 us -> 77.5 us  [per_device(): projected = lax.psum_scatter(partial, 'dp', scatter_dimension=0, tiled=True)]
    all_to_all x1 -> x0, starting transfers between devices: 4.59 us -> none  [per_device(): lax.all_to_all(projected, 'seq', 0, 0, tiled=True).reshape(row_count, -1)]
    ppermute x0 -> x3, starting transfers between devices: none -> 4.45 us  [pairwise_exchange(): lax.ppermute(sent, axis, [(i, i ^ step) for i in range(size)])]
  transfers between devices with their start and end apart: 10 -> 12, of which waited for: 8 -> 10; matrix products, arithmetic and copies ran while one was open for 8% -> 7% of each run, Pallas kernels for 0% -> 0%
where the time goes in v1:
time: 325 us; the launch traced here: 324 us
  waiting for transfers between devices  192 us (59%)
  blocking collectives  32.8 us (10%)
  starting transfers between devices  26.7 us (8%)
  matrix products  22.3 us (7%)
  other arithmetic  19.4 us (6%)
  local copies, waits for them, and re-layouts  16.4 us (5%)
  between operations  14.4 us (4%)
    reduce_scatter x1, waiting for transfers between devices, per_device(): projected = lax.psum_scatter(partial, 'dp', scatter_dimension=0, tiled=True)  77.5 us
    all_gather x1, waiting for transfers between devices, per_device(): gathered = lax.all_gather(weights, 'seq', axis=0, tiled=True)  57.2 us
    ppermute x6, waiting for transfers between devices, shift(): return (lax.ppermute(x, axis, pairs), reached)  30.4 us
    all_to_all x1, blocking collectives, per_device(): mine = lax.all_to_all(parts, 'dp', 0, 0, tiled=True)  30.4 us
    ppermute x3, waiting for transfers between devices, pairwise_exchange(): lax.ppermute(sent, axis, [(i, i ^ step) for i in range(size)])  24.1 us
    ppermute x6, starting transfers between devices, shift(): return (lax.ppermute(x, axis, pairs), reached)  19 us
    dot_general x1, matrix products, per_device(): partial = jnp.dot(mine, gathered, preferred_element_type=jnp.float32)  9.95 us
  transfers between devices with their start and end apart: 12, of which 10 were waited for; matrix products, arithmetic and copies ran while one was open for 7% of the time, Pallas kernels for 0%

profile of v1, /device:TPU:0, one launch (start us, length us, event | category | flops | bytes accessed | tf_op | source)
XLA Modules:
  0.0 324.2 jit_solution(13349305864751051352)
XLA Ops:
  7.4 2.4 pad_maximum_fusion
  9.8 3.3 %reshape_squeeze.4 = bf16[256,4,4,256]{3,2,1,0:T(4,128)(2,1)S(1)} reshape(bf16[1,256,4096]{2,1,0:T(8,128)(2,1)} %param.22) | data formatting | bytes 4194304 | tf_op jit(solution)/shard_map/reshape;squeeze | solution.py:89
  14.0 30.4 %all_to_all.14 = bf16[4,256,4,256]{3,2,1,0:T(4,128)(2,1)S(1)} all-to-all(bf16[4,256,4,256]{3,2,1,0:T(4,128)(2,1)S(1)} %bitcast.122), channel_id=1, replica_groups=mesh['grp'=1,'seq'=4,'dp'=4,'head'=2] {'dp'}, dimensions={0} | all-to-all | bytes 4194304 | tf_op jit(solution)/shard_map/all_to_all | solution.py:90
  44.8 57.2 %all-gather.2.cloned.1.call-done = bf16[1024,2192]{1,0:T(8,128)(2,1)} async-done(((bf16[256,2192]{1,0:T(8,128)(2,1)}), bf16[1024,2192]{1,0:T(8,128)(2,1)}) %all-gather.2.cloned.1.call-update) | async-done | bytes 4489232 | tf_op jit(solution)/shard_map/all_gather | solution.py:88
  102.0 10.0 %convolution_bitcast_fusion = f32[1024,2192]{0,1:T(8,128)} fusion(bf16[1024,2192]{1,0:T(8,128)(2,1)} %all-gather.2.cloned.1.call-done, bf16[1024,1024]{1,0:T(8,128)(2,1)S(1)} %bitcast.130), kind=kOutput, calls=%fused_computation.3 | convolution fusion | flops 4596957184 | bytes 15564800 | tf_op jit(solution)/shard_map/dot_general | solution.py:92
  114.0 3.2 all-to-all-start.1
  119.7 2.9 all-to-all-done.1
  124.2 77.5 %reduce-scatter.2.cloned.1.call-done = f32[256,2192]{0,1:T(8,128)} async-done(((f32[1024,2192]{0,1:T(8,128)}), f32[256,2192]{0,1:T(8,128)}) %reduce-scatter.2.cloned.1.call-update) | async-done | bytes 2244624 | tf_op jit(solution)/shard_map/reduce_scatter | solution.py:93
  201.7 1.7 convert_element_type.43
  204.3 3.4 %collective-permute-start.2 = (bf16[1,64,2192]{2,1,0:T(8,128)(2,1)S(1)}, bf16[1,64,2192]{2,1,0:T(8,128)(2,1)S(1)}, u32[]{:S(2)}, u32[]{:S(2)}) collective-permute-start(bf16[1,64,2192]{2,1,0:T(8,128)(2,1)S(1)} %get-tuple-element.80), channel_id=1, source_target_pairs={{0,24},{8,16},{16,8},{24,0},{1,25},{9,17},{17,9},{25,1},{2,26},{10... | collective-permute-start | bytes 841736 | tf_op jit(solution)/shard_map/ppermute | solution.py:27
  208.8 7.4 %collective-permute-done.2 = bf16[1,64,2192]{2,1,0:T(8,128)(2,1)S(1)} collective-permute-done((bf16[1,64,2192]{2,1,0:T(8,128)(2,1)S(1)}, bf16[1,64,2192]{2,1,0:T(8,128)(2,1)S(1)}, u32[]{:S(2)}, u32[]{:S(2)}) %collective-permute-start.2) | collective-permute-done | bytes 280608 | tf_op jit(solution)/shard_map/ppermute | solution.py:27
  216.1 16.7 %collective-permute-done.1 = bf16[1,64,2192]{2,1,0:T(8,128)(2,1)S(1)} collective-permute-done((bf16[1,64,2192]{2,1,0:T(8,128)(2,1)S(1)}, bf16[1,64,2192]{2,1,0:T(8,128)(2,1)S(1)}, u32[]{:S(2)}, u32[]{:S(2)}) %collective-permute-start.1) | collective-permute-done | bytes 280608 | tf_op jit(solution)/shard_map/ppermute | solution.py:27
  243.4 4.6 %collective-permute-start.3 = (f32[1032,128]{1,0:T(8,128)}, f32[1032,128]{1,0:T(8,128)S(1)}, u32[]{:S(2)}, u32[]{:S(2)}) collective-permute-start(f32[1032,128]{1,0:T(8,128)} %get-tuple-element.99), channel_id=1, source_target_pairs={{0,8},{8,16},{16,24},{1,9},{9,17},{17,25},{2,10},{10,18},{18,26},{... | collective-permute-start | bytes 1585160 | tf_op jit(solution)/shard_map/ppermute | solution.py:46
  249.0 8.2 %collective-permute-done.6 = f32[1032,128]{1,0:T(8,128)S(1)} collective-permute-done((f32[1032,128]{1,0:T(8,128)}, f32[1032,128]{1,0:T(8,128)S(1)}, u32[]{:S(2)}, u32[]{:S(2)}) %collective-permute-start.6) | collective-permute-done | bytes 528416 | tf_op jit(solution)/shard_map/ppermute | solution.py:46
  258.6 5.5 %collective-permute-start.4 = (f32[1032,128]{1,0:T(8,128)S(1)}, f32[1032,128]{1,0:T(8,128)}, u32[]{:S(2)}, u32[]{:S(2)}) collective-permute-start(f32[1032,128]{1,0:T(8,128)S(1)} %scatter.26), channel_id=1, source_target_pairs={{0,8},{8,16},{16,24},{1,9},{9,17},{17,25},{2,10},{10,18},{18,26},{... | collective-permute-start | bytes 1585160 | tf_op jit(solution)/shard_map/ppermute | solution.py:46
  264.2 5.7 %fusion = f32[16,128,256]{2,1,0:T(8,128)} fusion(bf16[256,16,128]{0,2,1:T(8,128)(2,1)S(1)} %bitcast.119, f32[16,256]{1,0:T(8,128)} %get-tuple-element.95, f32[256,256]{1,0:T(8,128)} %fusion.35, f32[16,256]{1,0:T(8,128)} %get-tuple-element.94, f32[256,256]{1,0:T(8,128)S(1)} %fusion.41), kind=kOutput, calls=%fused_computation.4 | convolution fusion | flops 1616904192 | bytes 3702784 | tf_op jit(solution)/shard_map/hts,shp->thp/dot_general | solution.py:125
  269.9 1.6 collective-permute-done.7
  275.8 5.0 %collective-permute-start.5 = (f32[1032,128]{1,0:T(8,128)}, f32[1032,128]{1,0:T(8,128)}, u32[]{:S(2)}, u32[]{:S(2)}) collective-permute-start(f32[1032,128]{1,0:T(8,128)} %pad_maximum_fusion.1), channel_id=1, source_target_pairs={{0,16},{8,24},{1,17},{9,25},{2,18},{10,26},{3,19},{11,27},{4,20},{... | collective-permute-start | bytes 1585160 | tf_op jit(solution)/shard_map/ppermute | solution.py:46
  285.0 4.2 %collective-permute-done.5 = f32[1032,128]{1,0:T(8,128)} collective-permute-done((f32[1032,128]{1,0:T(8,128)}, f32[1032,128]{1,0:T(8,128)}, u32[]{:S(2)}, u32[]{:S(2)}) %collective-permute-start.5) | collective-permute-done | bytes 528416 | tf_op jit(solution)/shard_map/ppermute | solution.py:46
  291.5 16.0 %collective-permute-done.8 = f32[1032,128]{1,0:T(8,128)S(1)} collective-permute-done((f32[1032,128]{1,0:T(8,128)S(1)}, f32[1032,128]{1,0:T(8,128)S(1)}, u32[]{:S(2)}, u32[]{:S(2)}) %collective-permute-start.8) | collective-permute-done | bytes 528416 | tf_op jit(solution)/shard_map/ppermute | solution.py:46
  307.6 2.6 multiply_reduce_fusion
  310.3 1.9 copy.100
  312.1 2.4 psum.7
  314.6 2.8 multiply_convert_fusion
  (106 shorter events, 33.1 us)
Async XLA Ops:
  6.5 95.5 %all-gather.2.cloned.1.call-start = ((), (), s32[]{:S(2)}) async-start(), calls=%async_computation.3 | async-start | bytes 5898240 | tf_op jit(solution)/shard_map/all_gather | solution.py:88
  9.8 192.0 %reduce-scatter.2.cloned.1.call-start = ((), (), s32[]{:S(2)}) async-start(), calls=%async_computation.4 | async-start | bytes 11223040 | tf_op jit(solution)/shard_map/reduce_scatter | solution.py:93
  112.0 0.7 copy-start.8
  112.0 5.2 %copy-start.9 = (s32[1,256]{1,0:T(1,128)S(1)}, s32[1,256]{1,0:T(1,128)}, u32[]{:S(2)}) copy-start(s32[1,256]{1,0:T(1,128)} %param.24) | copy-start | bytes 3076
  112.0 6.5 %copy-start.11 = (f32[16]{0:T(128)S(1)}, f32[16]{0:T(128)}, u32[]{:S(2)}) copy-start(f32[16]{0:T(128)} %param.29) | copy-start | bytes 196
  114.0 8.7 %all-to-all-start.1 = ((s32[4,1,64]{2,1,0:T(1,128)}), s32[4,1,64]{2,1,0:T(1,128)S(1)}, u32[]{:S(2)}, u32[]{:S(2)}) async-start(s32[4,1,64]{2,1,0:T(1,128)} %all_to_all.10), calls=%async_computation.2 | async-start | bytes 4096 | tf_op jit(solution)/shard_map/all_to_all | solution.py:96
  204.3 11.8 %collective-permute-start.2 = (bf16[1,64,2192]{2,1,0:T(8,128)(2,1)S(1)}, bf16[1,64,2192]{2,1,0:T(8,128)(2,1)S(1)}, u32[]{:S(2)}, u32[]{:S(2)}) collective-permute-start(bf16[1,64,2192]{2,1,0:T(8,128)(2,1)S(1)} %get-tuple-element.80), channel_id=1, source_target_pairs={{0,24},{8,16},{16,8},{24,0},{1,25},{9,17},{17,9},{25,1},{2,26},{10... | collective-permute-start | bytes 841736 | tf_op jit(solution)/shard_map/ppermute | solution.py:27
  207.7 25.1 %collective-permute-start.1 = (bf16[1,64,2192]{2,1,0:T(8,128)(2,1)S(1)}, bf16[1,64,2192]{2,1,0:T(8,128)(2,1)S(1)}, u32[]{:S(2)}, u32[]{:S(2)}) collective-permute-start(bf16[1,64,2192]{2,1,0:T(8,128)(2,1)S(1)} %get-tuple-element.81), channel_id=1, source_target_pairs={{0,16},{8,24},{16,0},{24,8},{1,17},{9,25},{17,1},{25,9},{2,18},{10... | collective-permute-start | bytes 841736 | tf_op jit(solution)/shard_map/ppermute | solution.py:27
  207.7 25.1 %collective-permute-start = (bf16[1,64,2192]{2,1,0:T(8,128)(2,1)S(1)}, bf16[1,64,2192]{2,1,0:T(8,128)(2,1)S(1)}, u32[]{:S(2)}, u32[]{:S(2)}) collective-permute-start(bf16[1,64,2192]{2,1,0:T(8,128)(2,1)S(1)} %get-tuple-element.82), channel_id=1, source_target_pairs={{0,8},{8,0},{16,24},{24,16},{1,9},{9,1},{17,25},{25,17},{2,10},{10... | collective-permute-start | bytes 841736 | tf_op jit(solution)/shard_map/ppermute | solution.py:27
  235.1 55.2 %copy-start = (bf16[256,2192]{1,0:T(8,128)(2,1)}, bf16[256,2192]{1,0:T(8,128)(2,1)S(1)}, u32[]{:S(2)}) copy-start(bf16[256,2192]{1,0:T(8,128)(2,1)S(1)} %gather_fusion.1) | copy-start | bytes 3366916
  235.1 0.7 copy-start.7
  242.1 15.2 %collective-permute-start.6 = (f32[1032,128]{1,0:T(8,128)}, f32[1032,128]{1,0:T(8,128)S(1)}, u32[]{:S(2)}, u32[]{:S(2)}) collective-permute-start(f32[1032,128]{1,0:T(8,128)} %get-tuple-element.98), channel_id=1, source_target_pairs={{8,0},{16,8},{24,16},{9,1},{17,9},{25,17},{10,2},{18,10},{26,18},{... | collective-permute-start | bytes 1585160 | tf_op jit(solution)/shard_map/ppermute | solution.py:46
  243.4 15.2 %collective-permute-start.3 = (f32[1032,128]{1,0:T(8,128)}, f32[1032,128]{1,0:T(8,128)S(1)}, u32[]{:S(2)}, u32[]{:S(2)}) collective-permute-start(f32[1032,128]{1,0:T(8,128)} %get-tuple-element.99), channel_id=1, source_target_pairs={{0,8},{8,16},{16,24},{1,9},{9,17},{17,25},{2,10},{10,18},{18,26},{... | collective-permute-start | bytes 1585160 | tf_op jit(solution)/shard_map/ppermute | solution.py:46
  257.3 12.6 %copy-start.3 = (f32[1032,128]{1,0:T(8,128)}, f32[1032,128]{1,0:T(8,128)S(1)}, u32[]{:S(2)}) copy-start(f32[1032,128]{1,0:T(8,128)S(1)} %scatter.30) | copy-start | bytes 1585156
  257.3 14.2 %collective-permute-start.7 = (f32[1032,128]{1,0:T(8,128)S(1)}, f32[1032,128]{1,0:T(8,128)}, u32[]{:S(2)}, u32[]{:S(2)}) collective-permute-start(f32[1032,128]{1,0:T(8,128)S(1)} %scatter.30), channel_id=1, source_target_pairs={{8,0},{16,8},{24,16},{9,1},{17,9},{25,17},{10,2},{18,10},{26,18},{... | collective-permute-start | bytes 1585160 | tf_op jit(solution)/shard_map/ppermute | solution.py:46
  258.6 11.2 %copy-start.2 = (f32[1032,128]{1,0:T(8,128)}, f32[1032,128]{1,0:T(8,128)S(1)}, u32[]{:S(2)}) copy-start(f32[1032,128]{1,0:T(8,128)S(1)} %scatter.26) | copy-start | bytes 1585156
  258.6 14.0 %collective-permute-start.4 = (f32[1032,128]{1,0:T(8,128)S(1)}, f32[1032,128]{1,0:T(8,128)}, u32[]{:S(2)}, u32[]{:S(2)}) collective-permute-start(f32[1032,128]{1,0:T(8,128)S(1)} %scatter.26), channel_id=1, source_target_pairs={{0,8},{8,16},{16,24},{1,9},{9,17},{17,25},{2,10},{10,18},{18,26},{... | collective-permute-start | bytes 1585160 | tf_op jit(solution)/shard_map/ppermute | solution.py:46
  275.8 13.4 %collective-permute-start.5 = (f32[1032,128]{1,0:T(8,128)}, f32[1032,128]{1,0:T(8,128)}, u32[]{:S(2)}, u32[]{:S(2)}) collective-permute-start(f32[1032,128]{1,0:T(8,128)} %pad_maximum_fusion.1), channel_id=1, source_target_pairs={{0,16},{8,24},{1,17},{9,25},{2,18},{10,26},{3,19},{11,27},{4,20},{... | collective-permute-start | bytes 1585160 | tf_op jit(solution)/shard_map/ppermute | solution.py:46
  282.4 25.2 %collective-permute-start.8 = (f32[1032,128]{1,0:T(8,128)S(1)}, f32[1032,128]{1,0:T(8,128)S(1)}, u32[]{:S(2)}, u32[]{:S(2)}) collective-permute-start(f32[1032,128]{1,0:T(8,128)S(1)} %pad_maximum_fusion.2), channel_id=1, source_target_pairs={{16,0},{24,8},{17,1},{25,9},{18,2},{26,10},{19,3},{27,11},{20,4},{... | collective-permute-start | bytes 1585160 | tf_op jit(solution)/shard_map/ppermute | solution.py:46
  290.3 17.3 %copy-start.1 = (f32[16,128,256]{2,1,0:T(8,128)S(1)}, f32[16,128,256]{2,1,0:T(8,128)}, u32[]{:S(2)}) copy-start(f32[16,128,256]{2,1,0:T(8,128)} %fusion) | copy-start | bytes 6291460
  290.3 17.3 %copy-start.4 = (f32[256,16]{0,1:T(8,128)S(1)}, f32[256,16]{0,1:T(8,128)}, u32[]{:S(2)}) copy-start(f32[256,16]{0,1:T(8,128)} %get-tuple-element.74) | copy-start | bytes 49156
  290.3 17.3 %copy-start.5 = (f32[256,16]{0,1:T(8,128)S(1)}, f32[256,16]{0,1:T(8,128)}, u32[]{:S(2)}) copy-start(f32[256,16]{0,1:T(8,128)} %get-tuple-element.90) | copy-start | bytes 49156
  290.3 17.3 %copy-start.10 = (f32[16]{0:T(128)S(1)}, f32[16]{0:T(128)}, u32[]{:S(2)}) copy-start(f32[16]{0:T(128)} %param.30) | copy-start | bytes 196
  310.2 4.3 %copy-start.6 = (f32[2048]{0:T(1024)S(1)}, f32[2048]{0:T(1024)}, u32[]{:S(2)}) copy-start(f32[2048]{0:T(1024)} %param.31) | copy-start | bytes 24580
Sparse Core Ops, SparseCore 0:
  9.9 92.0 all-gather.1
  112.1 89.5 reduce-scatter.1
